TPU v7x, 128 devices: a whole 4x4x4 slice. The times are simulated.
128 devices in a mesh: ctl: 32 (over y, z_lo, x), side: 2 (over core), tp: 2 (over z_hi).
Axes of the slice: x: 4, y: 4, z: 4 (z_hi: 2, z_lo: 2; z = z_hi * 2 + z_lo), core: 2. Of those that a mesh axis runs over, the one named last changes fastest.
Arguments:
- image_latent: bfloat16 [64, 256, 3072], P('ctl'), may hold values from -6 to 6
- control_latent: bfloat16 [64, 256, 3072], P('ctl'), may hold values from -6 to 6
- control_order: int32 [64, 256], P('ctl'), may hold values from 0 to 255, each once within a row
- captions: bfloat16 [128, 128, 3072], P('ctl'), may hold values from -6 to 6
- caption_ids: int32 [64], P('ctl'), may hold values from 0 to 3
- modulation: float32 [2, 64, 3, 3072], P('side', 'ctl'), may hold values from -3 to 3
- qkv_weight: bfloat16 [2, 3072, 3, 1536], P('side', 'ctl', None, 'tp'), may hold values from -1 to 1
- qk_gain: float32 [2, 2, 128], P('side'), may hold values from 1 to 6
- out_weight: bfloat16 [2, 1536, 3072], P('side', 'tp', 'ctl'), may hold values from -0.5 to 0.5
- zero_weight: bfloat16 [3072, 3072], P('ctl', 'tp'), may hold values from -0.109375 to 0.109375
- proj_weight: bfloat16 [3072, 64], P('tp'), may hold values from -1 to 1
- final_mod: float32 [64, 2, 3072], P('ctl'), may hold values from -3 to 3
- velocity_target: float32 [64, 256, 64], P('ctl'), may hold values from -6 to 6
Outputs:
- hidden_out: bfloat16 [2, 64, 256, 3072], P('side', 'ctl', None, 'tp')
- zero_grad: float32 [3072, 3072], P(('ctl', 'side'), 'tp')
Inputs may be any that keep to these rules, and one draw needn't show every extreme that they name: caption_ids counts from the first caption held by the sample's own index of ctl. Each sample's row of control_order is a permutation.
All inputs are finite; a program needn't handle non-finite values.
Results may differ from a plain program's by a relative error of at most 0.03.
Values may be sent and summed in bfloat16 or wider, within the bound.
No kernel may reach another device: no remote copies, remote signals or barrier semaphores. Data moves between devices by JAX's collectives and lax.ppermute only.
A program may use at most 192 MiB of HBM per device.

v0:
```python
import math
import jax
import jax.numpy as jnp
from jax import lax
from jax.sharding import PartitionSpec as P

HEAD_DIM = 128
EPS = 1e-06


def passed_along(shard, axis, by):
    length = lax.axis_size(axis)
    pairs = [(i, i + by) for i in range(length) if 0 <= i + by < length]
    return lax.ppermute(shard, axis, pairs)


def partner(value, axis, bit):
    mask = 2**bit
    pairs = [(source, source ^ mask) for source in range(lax.axis_size(axis))]
    return lax.ppermute(value, axis, pairs)


def swap(value, axis):
    return lax.ppermute(value, axis, [(0, 1), (1, 0)])


def layer_norm(values):
    center = values - jnp.mean(values, axis=-1, keepdims=True)
    spread = jnp.mean(center * center, axis=-1, keepdims=True)
    return center * lax.rsqrt(spread + EPS)


def head_norm(values, gain_row):
    power_mean = jnp.mean(values * values, axis=-1, keepdims=True)
    return (values * lax.rsqrt(power_mean + EPS) * gain_row).astype(jnp.bfloat16)


def rounded(values):
    narrow = lax.optimization_barrier(values.astype(jnp.bfloat16))
    return narrow.astype(jnp.float32)


def local(
    image_latent,
    control_latent,
    control_order,
    captions,
    caption_ids,
    modulation,
    qkv_weight,
    qk_gain,
    out_weight,
    zero_weight,
    proj_weight,
    final_mod,
    velocity_target,
):
    side_index = lax.axis_index("side")
    tp_index = lax.axis_index("tp")
    ctl_count = lax.axis_size("ctl")
    tp_count = lax.axis_size("tp")
    is_control = side_index == 0
    micro_count, img_rows, width_full = image_latent.shape
    text_rows = captions.shape[1]
    seq_rows = text_rows + img_rows
    local_heads = qkv_weight.shape[3]
    head_count = local_heads // HEAD_DIM
    half_width = width_full // tp_count
    quarter_width = half_width // 2
    flat_rows = micro_count * img_rows
    block_rows = width_full // (2 * ctl_count)
    aligned = jax.vmap(lambda latent, order_row: jnp.take(latent, order_row, axis=0))(
        control_latent, control_order
    )
    plain_rows = image_latent.astype(jnp.float32)
    hidden = plain_rows + jnp.where(is_control, 1.0, 0.0) * aligned.astype(jnp.float32)
    chosen = jnp.take(captions, caption_ids, axis=0).astype(jnp.float32)
    sequence = jnp.concatenate([chosen, hidden], axis=1)
    modulate = modulation[0]
    normed = (layer_norm(sequence) * (1.0 + modulate[:, 1:2]) + modulate[:, 0:1]).astype(
        jnp.bfloat16
    )
    text_flat = normed.reshape(micro_count * seq_rows, width_full)
    image_flat = normed[:, text_rows:].reshape(flat_rows, width_full)
    local_rows = qkv_weight.shape[1]
    own_cols = lax.dynamic_slice_in_dim(zero_weight, side_index * quarter_width, quarter_width, 1)
    packed = jnp.concatenate(
        [qkv_weight[0].reshape(local_rows, 3 * local_heads), out_weight[0].T, own_cols], axis=1
    )
    gathered = lax.all_gather(packed, "ctl", axis=0, tiled=True)
    count_rows = gathered.shape[0]
    query_weight = gathered[:, :local_heads]
    pair_weight = gathered[:, local_heads : 3 * local_heads]
    out_cols = gathered[:, 3 * local_heads : 4 * local_heads]
    zero_cols = gathered[:, 4 * local_heads :]
    query_acc = jnp.dot(image_flat, query_weight, preferred_element_type=jnp.float32)
    pair_acc = jnp.dot(text_flat, pair_weight, preferred_element_type=jnp.float32)
    gain_pair = qk_gain[0]
    queries = head_norm(
        query_acc.reshape(micro_count, img_rows, head_count, HEAD_DIM), gain_pair[0]
    )
    pair_acc = pair_acc.reshape(micro_count, seq_rows, 2, head_count, HEAD_DIM)
    keys_all = head_norm(pair_acc[:, :, 0], gain_pair[1])
    values_all = pair_acc[:, :, 1].astype(jnp.bfloat16)
    scores = jnp.einsum(
        "bihd,bjhd->bhij", queries, keys_all, preferred_element_type=jnp.float32
    ) / math.sqrt(HEAD_DIM)
    attend = jax.nn.softmax(scores, axis=-1).astype(jnp.bfloat16)
    mixed_heads = jnp.einsum(
        "bhij,bjhd->bihd", attend, values_all, preferred_element_type=jnp.float32
    )
    mixed_heads = mixed_heads.astype(jnp.bfloat16).reshape(flat_rows, local_heads)
    contract_last = (((1,), (1,)), ((), ()))
    other_out = lax.dynamic_slice_in_dim(out_cols, (1 - tp_index) * half_width, half_width, 0)
    own_out = lax.dynamic_slice_in_dim(out_cols, tp_index * half_width, half_width, 0)
    other_part = lax.dot_general(
        mixed_heads, other_out, contract_last, preferred_element_type=jnp.float32
    ).astype(jnp.bfloat16)
    got_part = swap(other_part, "tp")
    own_part_heads = rounded(
        lax.dot_general(mixed_heads, own_out, contract_last, preferred_element_type=jnp.float32)
    )
    head_sum = own_part_heads + got_part.astype(jnp.float32)
    hid_half = lax.dynamic_slice_in_dim(hidden, tp_index * half_width, half_width, 2)
    gate_half = lax.dynamic_slice_in_dim(modulate[:, 2:3], tp_index * half_width, half_width, 2)
    act_half = hid_half + gate_half * head_sum.reshape(micro_count, img_rows, half_width)
    act_half = act_half.reshape(flat_rows, half_width)
    act_own = act_half.astype(jnp.bfloat16)
    act_got = swap(act_own, "tp")
    act_narrow = jnp.where(
        tp_index == 0,
        jnp.concatenate([act_own, act_got], axis=1),
        jnp.concatenate([act_got, act_own], axis=1),
    )
    act_other = passed_along(act_narrow, "side", 1)
    control_rows = jnp.where(is_control, act_narrow, act_other)
    own_part = jnp.dot(control_rows, zero_cols, preferred_element_type=jnp.float32)
    own_narrow = own_part.astype(jnp.bfloat16)
    other_narrow = partner(own_narrow, "side", 0)
    residual_narrow = jnp.where(
        is_control,
        jnp.concatenate([own_narrow, other_narrow], axis=1),
        jnp.concatenate([other_narrow, own_narrow], axis=1),
    )
    merged = act_half + residual_narrow.astype(jnp.float32)
    section_out = jnp.where(is_control, residual_narrow, merged.astype(jnp.bfloat16))
    final_half = lax.dynamic_slice_in_dim(final_mod, tp_index * half_width, half_width, 2)
    merged_rows = merged.reshape(micro_count, img_rows, half_width)
    row_total, squares = lax.psum(
        (
            jnp.sum(merged_rows, axis=-1, keepdims=True),
            jnp.sum(merged_rows * merged_rows, axis=-1, keepdims=True),
        ),
        "tp",
    )
    mean_val = row_total / width_full
    spread = squares / width_full - mean_val * mean_val
    scale_inv = lax.rsqrt(spread + EPS)
    unit_rows = (merged_rows - mean_val) * scale_inv
    final_in = (unit_rows * (1.0 + final_half[:, 1:2]) + final_half[:, 0:1]).astype(jnp.bfloat16)
    pred_part = jnp.dot(
        final_in.reshape(flat_rows, half_width), proj_weight, preferred_element_type=jnp.float32
    )
    prediction = pred_part + swap(pred_part, "tp")
    loss_factor = 4.0 / math.sqrt(micro_count * ctl_count * img_rows)
    grad_pred = (loss_factor * (prediction - velocity_target.reshape(flat_rows, -1))).astype(
        jnp.bfloat16
    )
    grad_unit = lax.dot_general(
        grad_pred, proj_weight, (((1,), (1,)), ((), ())), preferred_element_type=jnp.float32
    )
    grad_unit = grad_unit.reshape(micro_count, img_rows, half_width) * (1.0 + final_half[:, 1:2])
    first_sum, second_sum = lax.psum(
        (
            jnp.sum(grad_unit, axis=-1, keepdims=True),
            jnp.sum(grad_unit * unit_rows, axis=-1, keepdims=True),
        ),
        "tp",
    )
    grad_narrow = (
        (grad_unit - first_sum / width_full - unit_rows * (second_sum / width_full)) * scale_inv
    ).astype(jnp.bfloat16)
    grad_narrow = grad_narrow.reshape(flat_rows, half_width)
    returned = passed_along(grad_narrow, "side", -1)
    grad_rows_all = jnp.where(is_control, returned, grad_narrow)
    own_act = lax.dynamic_index_in_dim(
        control_rows.reshape(flat_rows, ctl_count, 2, block_rows), side_index, 2, keepdims=False
    )
    own_act = own_act.reshape(flat_rows, ctl_count * block_rows)
    product = lax.dot_general(
        own_act, grad_rows_all, (((0,), (0,)), ((), ())), preferred_element_type=jnp.float32
    )
    group_parts = rounded(product).astype(jnp.bfloat16).reshape(ctl_count, block_rows, half_width)
    received = lax.all_to_all(group_parts, "ctl", 0, 0, tiled=True)
    zero_grad = jnp.sum(received.astype(jnp.float32), axis=0)
    return (section_out.reshape(1, micro_count, img_rows, half_width), zero_grad)


def solution(mesh):
    return jax.shard_map(
        local,
        mesh=mesh,
        in_specs=(
            P("ctl", None, None),
            P("ctl", None, None),
            P("ctl", None),
            P("ctl", None, None),
            P("ctl"),
            P("side", "ctl", None, None),
            P("side", "ctl", None, "tp"),
            P("side", None, None),
            P("side", "tp", "ctl"),
            P("ctl", "tp"),
            P("tp", None),
            P("ctl", None, None),
            P("ctl", None, None),
        ),
        out_specs=(P("side", "ctl", None, "tp"), P(("ctl", "side"), "tp")),
        check_vma=False,
    )
```

profile of v0, /device:TPU:113, one launch (start us, length us, event | category | flops | bytes accessed | tf_op | source)
XLA Modules:
  0.0 585.1 jit_solution(12119574096527699242)
XLA Ops:
  7.2 1.5 copy.20
  8.8 0.8 copy.38
  9.6 0.9 constant_dynamic-slice_fusion.2
  10.5 2.0 pad_maximum_fusion.1
  12.6 14.8 %gather_fusion.1 = bf16[512,3072]{1,0:T(8,128)(2,1)} fusion(bf16[2,256,3072]{2,1,0:T(8,128)(2,1)S(1)} %copy-done, s32[512]{0:T(512)S(1)} %bitcast.109), kind=kCustom, calls=%fused_computation.1 | custom fusion | bytes 6295552 | tf_op jit(solution)/shard_map/vmap(jit(_take))/gather | solution.py:72
  27.4 3.7 gather_fusion
  31.2 1.7 select_convert_fusion
  32.9 4.4 multiply_add_fusion
  37.3 0.6 fusion.1
  38.0 1.3 multiply_reduce_fusion
  39.3 0.7 copy-done.2
  40.0 3.6 add_convert_fusion
  43.6 228.4 %all-gather.2.cloned.1.call-done = bf16[3072,3840]{1,0:T(8,128)(2,1)} async-done(((bf16[96,3840]{1,0:T(8,128)(2,1)}), bf16[3072,3840]{1,0:T(8,128)(2,1)}) %all-gather.2.cloned.1.call-update) | async-done | bytes 23592976 | tf_op jit(solution)/shard_map/all_gather | solution.py:90
  272.0 8.0 %slice_bitcast_fusion = bf16[1536,3072]{0,1:T(8,128)(2,1)} fusion(bf16[3072,3840]{1,0:T(8,128)(2,1)} %all-gather.2.cloned.1.call-done), kind=kLoop, calls=%fused_computation.3 | loop fusion | bytes 18874368 | tf_op jit(solution)/shard_map/dot_general | solution.py:97
  280.0 12.6 %copy.21 = bf16[1536,3072]{1,0:T(8,128)(2,1)} copy(bf16[1536,3072]{0,1:T(8,128)(2,1)} %slice_bitcast_fusion) | data formatting | bytes 18874368 | tf_op jit(solution)/shard_map/dot_general | solution.py:97
  292.7 11.5 %fusion.4 = f32[2,384,2,6,128]{1,4,3,2,0:T(8,128)S(1)} fusion(bf16[2,6,128,3072,1]{3,2,1,0,4:T(8,128)(2,1)} %bitcast.113, bf16[2,384,3072]{2,1,0:T(8,128)(2,1)} %add_convert_fusion), kind=kOutput, calls=%fused_computation.14 | convolution fusion | flops 7247757312 | bytes 18874368 | tf_op jit(solution)/shard_map/dot_general | solution.py:97
  304.2 2.1 copy-done.9
  306.3 0.2 multiply_reduce_fusion.4
  306.6 8.2 %fusion.46 = (bf16[3072,768]{1,0:T(8,128)(2,1)}, bf16[768,3072]{0,1:T(8,128)(2,1)}) fusion(bf16[3072,3840]{1,0:T(8,128)(2,1)} %all-gather.2.cloned.1.call-done), kind=kLoop, calls=%fused_computation.99 | loop fusion | bytes 18874368 | tf_op jit(solution)/shard_map/slice | solution.py:94
  314.7 6.7 %copy.22 = bf16[768,3072]{1,0:T(8,128)(2,1)} copy(bf16[768,3072]{0,1:T(8,128)(2,1)} %get-tuple-element.10) | data formatting | bytes 9437184 | tf_op jit(solution)/shard_map/dot_general | solution.py:96
  321.4 6.0 %multiply_reduce_fusion.5 = (f32[2,256,6]{1,2,0:T(8,128)S(1)}, f32[2,256,6,128]{1,3,2,0:T(8,128)S(1)}) fusion(bf16[6,128,3072,1]{2,1,0,3:T(8,128)(2,1)} %bitcast.118, bf16[2,384,3072]{2,1,0:T(8,128)(2,1)} %add_convert_fusion), kind=kOutput, calls=%fused_computation.48 | convolution fusion | flops 2416702464 | bytes 9449472 | tf_op jit(solution)/shard_map/dot_general | solution.py:96
  327.4 2.6 fusion.22
  330.0 2.2 copy-done.4
  332.1 1.7 fusion.48
  333.9 10.0 %fusion.21 = bf16[2,256,6,128]{1,3,2,0:T(8,128)(2,1)S(1)} fusion(f32[2,6,256]{2,1,0:T(8,128)S(1)} %fusion.48, f32[2,384,2,6,128]{1,4,3,2,0:T(8,128)} %copy-done.9, f32[2,6,256,384]{3,2,1,0:T(8,128)} %copy-done.4), kind=kOutput, calls=%fused_computation.53 | convolution fusion | flops 308284800 | bytes 11415552 | tf_op jit(solution)/shard_map/bhij,bjhd->bihd/dot_general | solution.py:109
  343.9 0.8 copy.25
  344.7 0.2 copy.39
  344.9 3.1 convolution_convert_fusion.1
  348.0 1.0 collective-permute-start
  349.0 3.1 convolution_convert_fusion.2
  352.1 32.9 %collective-permute-done = bf16[512,1536]{1,0:T(8,128)(2,1)} collective-permute-done((bf16[512,1536]{1,0:T(8,128)(2,1)S(1)}, bf16[512,1536]{1,0:T(8,128)(2,1)}, u32[]{:S(2)}, u32[]{:S(2)}) %collective-permute-start) | collective-permute-done | bytes 1572896 | tf_op jit(solution)/shard_map/ppermute | solution.py:24
  385.0 1.8 convert_add_fusion.1
  386.8 4.9 fusion.27
  391.8 1.7 copy.27
  393.5 0.8 collective-permute-start.1
  394.3 0.3 copy-done.8
  394.6 34.8 %collective-permute-done.1 = bf16[512,1536]{0,1:T(8,128)(2,1)} collective-permute-done((bf16[512,1536]{0,1:T(8,128)(2,1)S(1)}, bf16[512,1536]{0,1:T(8,128)(2,1)}, u32[]{:S(2)}, u32[]{:S(2)}) %collective-permute-start.1) | collective-permute-done | bytes 1572896 | tf_op jit(solution)/shard_map/ppermute | solution.py:24
  429.4 3.2 maximum_select_fusion
  432.6 1.3 collective-permute-start.2
  433.9 7.7 %collective-permute-done.2 = bf16[512,3072]{0,1:T(8,128)(2,1)S(1)} collective-permute-done((bf16[512,3072]{0,1:T(8,128)(2,1)S(1)}, bf16[512,3072]{0,1:T(8,128)(2,1)S(1)}, u32[]{:S(2)}, u32[]{:S(2)}) %collective-permute-start.2) | collective-permute-done | bytes 3145760 | tf_op jit(solution)/shard_map/ppermute | solution.py:14
  441.6 0.4 broadcast_select_fusion
  442.0 6.1 %fusion.18 = bf16[512,768]{1,0:T(8,128)(2,1)S(1)} fusion(bf16[512,3072]{0,1:T(8,128)(2,1)S(1)} %broadcast_select_fusion, bf16[3072,3840]{1,0:T(8,128)(2,1)} %all-gather.2.cloned.1.call-done), kind=kOutput, calls=%fused_computation.52 | convolution fusion | flops 2416312320 | bytes 8650752 | tf_op jit(solution)/shard_map/dot_general | solution.py:137
  448.2 0.2 collective-permute-start.3
  448.6 2.0 collective-permute-done.3
  450.6 0.9 copy-done.11
  451.5 4.3 fusion.45
  455.8 5.4 all-reduce.1
  461.3 0.7 add_convert_fusion.1
  461.9 0.6 fusion.49
  462.5 0.9 collective-permute-start.4
  463.4 4.5 collective-permute-done.4
  467.9 0.7 fusion.10
  468.6 0.6 multiply_reduce_fusion.2
  469.3 1.0 copy-done.5
  470.3 5.3 all-reduce
  475.6 4.0 multiply_convert_fusion
  479.6 5.8 collective-permute-start.5
  485.4 1.5 constant_dynamic-slice_fusion.1
  486.9 1.4 collective-permute-done.5
  488.3 5.7 convolution_convert_fusion
  494.0 7.7 %all-to-all-start = ((bf16[32,48,1536]{2,1,0:T(8,128)(2,1)}), bf16[32,48,1536]{2,1,0:T(8,128)(2,1)}, u32[]{:S(2)}, u32[]{:S(2)}) async-start(bf16[32,48,1536]{2,1,0:T(8,128)(2,1)} %bitcast.117), calls=%async_computation | async-start | bytes 9437184 | tf_op jit(solution)/shard_map/all_to_all | solution.py:194
  501.7 4.7 select_bitcast_fusion
  506.4 67.9 %all-to-all-done = bf16[32,48,1536]{2,1,0:T(8,128)(2,1)} async-done(((bf16[32,48,1536]{2,1,0:T(8,128)(2,1)}), bf16[32,48,1536]{2,1,0:T(8,128)(2,1)}, u32[]{:S(2)}, u32[]{:S(2)}) %all-to-all-start) | async-done | bytes 4718624 | tf_op jit(solution)/shard_map/all_to_all | solution.py:194
  574.3 3.7 convert_reduce_fusion
  (54 shorter events, 0.4 us)
Async XLA Ops:
  7.2 5.5 copy-start
  7.2 5.4 copy-start.16
  7.2 264.8 %all-gather.2.cloned.1.call-start = ((), (), s32[]{:S(2)}) async-start(), calls=%async_computation.1 | async-start | bytes 24330240 | tf_op jit(solution)/shard_map/all_gather | solution.py:90
  12.6 14.8 %copy-start.18 = (s32[2]{0:T(128)S(1)}, s32[2]{0:T(128)}, u32[]{:S(2)}) copy-start(s32[2]{0:T(128)} %param.17) | copy-start | bytes 28
  27.4 3.7 copy-start.17
  37.3 2.7 copy-start.2
  38.0 1.3 copy-start.14
  304.2 2.2 copy-start.9
  329.9 2.2 copy-start.4
  348.0 37.0 %collective-permute-start = (bf16[512,1536]{1,0:T(8,128)(2,1)S(1)}, bf16[512,1536]{1,0:T(8,128)(2,1)}, u32[]{:S(2)}, u32[]{:S(2)}) collective-permute-start(bf16[512,1536]{1,0:T(8,128)(2,1)S(1)} %convolution_convert_fusion.1), channel_id=1, source_target_pairs={{0,1},{1,0},{2,3},{3,2},{4,5},{5,4},{6,7},{7,6},{8,9},{9,8},{10,11... | collective-permute-start | bytes 4718600 | tf_op jit(solution)/shard_map/ppermute | solution.py:24
  386.8 4.9 copy-start.6
  393.5 1.1 copy-start.8
  393.5 35.9 %collective-permute-start.1 = (bf16[512,1536]{0,1:T(8,128)(2,1)S(1)}, bf16[512,1536]{0,1:T(8,128)(2,1)}, u32[]{:S(2)}, u32[]{:S(2)}) collective-permute-start(bf16[512,1536]{0,1:T(8,128)(2,1)S(1)} %copy.27), channel_id=1, source_target_pairs={{0,1},{1,0},{2,3},{3,2},{4,5},{5,4},{6,7},{7,6},{8,9},{9,8},{10,11... | collective-permute-start | bytes 4718600 | tf_op jit(solution)/shard_map/ppermute | solution.py:24
  432.6 9.0 %collective-permute-start.2 = (bf16[512,3072]{0,1:T(8,128)(2,1)S(1)}, bf16[512,3072]{0,1:T(8,128)(2,1)S(1)}, u32[]{:S(2)}, u32[]{:S(2)}) collective-permute-start(bf16[512,3072]{0,1:T(8,128)(2,1)S(1)} %maximum_select_fusion), channel_id=1, source_target_pairs={{0,2},{1,3},{4,6},{5,7},{8,10},{9,11},{12,14},{13,15},{16,18},{17,... | collective-permute-start | bytes 9437192 | tf_op jit(solution)/shard_map/ppermute | solution.py:14
  442.0 6.2 %copy-start.7 = (bf16[512,3072]{0,1:T(8,128)(2,1)}, bf16[512,3072]{0,1:T(8,128)(2,1)S(1)}, u32[]{:S(2)}) copy-start(bf16[512,3072]{0,1:T(8,128)(2,1)S(1)} %broadcast_select_fusion) | copy-start | bytes 9437188
  442.0 6.4 %copy-start.15 = (f32[2,2,3072]{2,1,0:T(2,128)S(1)}, f32[2,2,3072]{2,1,0:T(2,128)}, u32[]{:S(2)}) copy-start(f32[2,2,3072]{2,1,0:T(2,128)} %param.24) | copy-start | bytes 147460
  448.2 2.4 copy-start.10
  448.2 2.4 collective-permute-start.3
  450.6 0.9 copy-start.11
  455.8 19.8 %copy-start.3 = (f32[2,256,1536]{2,1,0:T(8,128)}, f32[2,256,1536]{2,1,0:T(8,128)S(1)}, u32[]{:S(2)}) copy-start(f32[2,256,1536]{2,1,0:T(8,128)S(1)} %get-tuple-element.8) | copy-start | bytes 9437188
  455.8 6.1 %copy-start.12 = (bf16[1536,64]{0,1:T(8,128)(2,1)S(1)}, bf16[1536,64]{0,1:T(8,128)(2,1)}, u32[]{:S(2)}) copy-start(bf16[1536,64]{0,1:T(8,128)(2,1)} %param.23) | copy-start | bytes 589828
  461.3 2.1 copy-start.13
  462.5 5.4 collective-permute-start.4
  468.6 1.7 copy-start.5
  479.6 8.7 %collective-permute-start.5 = (bf16[512,1536]{1,0:T(8,128)(2,1)}, bf16[512,1536]{1,0:T(8,128)(2,1)S(1)}, u32[]{:S(2)}, u32[]{:S(2)}) collective-permute-start(bf16[512,1536]{1,0:T(8,128)(2,1)} %bitcast.40), channel_id=1, source_target_pairs={{2,0},{3,1},{6,4},{7,5},{10,8},{11,9},{14,12},{15,13},{18,16},{19,... | collective-permute-start | bytes 4718600 | tf_op jit(solution)/shard_map/ppermute | solution.py:14
  494.0 80.3 %all-to-all-start = ((bf16[32,48,1536]{2,1,0:T(8,128)(2,1)}), bf16[32,48,1536]{2,1,0:T(8,128)(2,1)}, u32[]{:S(2)}, u32[]{:S(2)}) async-start(bf16[32,48,1536]{2,1,0:T(8,128)(2,1)} %bitcast.117), calls=%async_computation | async-start | bytes 9437184 | tf_op jit(solution)/shard_map/all_to_all | solution.py:194
  501.7 76.4 %copy-start.1 = (bf16[2,256,3072]{2,1,0:T(8,128)(2,1)S(1)}, bf16[2,256,3072]{2,1,0:T(8,128)(2,1)}, u32[]{:S(2)}) copy-start(bf16[2,256,3072]{2,1,0:T(8,128)(2,1)} %param.14) | copy-start | bytes 9437188
Sparse Core Ops, SparseCore 0:
  12.7 259.2 all-gather.1
where the time goes:
time: 595 us; the launch traced here: 585 us
  waiting for transfers between devices  380 us (64%)
  local copies, waits for them, and re-layouts  68.8 us (12%)
  matrix products  49.4 us (8%)
  other arithmetic  44.1 us (7%)
  starting transfers between devices  17.6 us (3%)
  between operations  14.7 us (2%)
  blocking collectives  10.7 us (2%)
    all_gather x1, waiting for transfers between devices, local(): gathered = lax.all_gather(packed, 'ctl', axis=0, tiled=True)  228 us
    ppermute x3, waiting for transfers between devices, swap(): return lax.ppermute(value, axis, [(0, 1), (1, 0)])  72.2 us
    all_to_all x1, waiting for transfers between devices, local(): received = lax.all_to_all(group_parts, 'ctl', 0, 0, tiled=True)  67.9 us
    dot_general x2, local copies, waits for them, and re-layouts, local(): jnp.dot(text_flat, pair_weight, preferred_element_type=jnp.float32)  20.7 us
    gather x1, local copies, waits for them, and re-layouts, local(): jnp.take(latent, order_row, axis=0)  14.8 us
  transfers between devices with their start and end apart: 8, of which 8 were waited for; matrix products, arithmetic and copies ran while one was open for 7% of the time, Pallas kernels for 0%

commit v1 on v0

--- a/solution.py
+++ b/solution.py
@@ -87,7 +87,9 @@
     packed = jnp.concatenate(
         [qkv_weight[0].reshape(local_rows, 3 * local_heads), out_weight[0].T, own_cols], axis=1
     )
-    gathered = lax.all_gather(packed, "ctl", axis=0, tiled=True)
+    gathered = jnp.concatenate(
+        lax.all_to_all(jnp.stack([packed] * lax.axis_size("ctl")), "ctl", 0, 0), axis=0
+    )
     count_rows = gathered.shape[0]
     query_weight = gathered[:, :local_heads]
     pair_weight = gathered[:, local_heads : 3 * local_heads]

time: 595 us -> 768 us (1.29)
  the two profiles are of different devices: /device:TPU:113 before, /device:TPU:69 now
where the time goes in v1:
time: 768 us; the launch traced here: 757 us
  waiting for transfers between devices  492 us (64%)
  starting transfers between devices  84.8 us (11%)
  local copies, waits for them, and re-layouts  77.1 us (10%)
  matrix products  48 us (6%)
  other arithmetic  43.4 us (6%)
  blocking collectives  10.7 us (1%)
    all_to_all x1, waiting for transfers between devices, local(): lax.all_to_all(jnp.stack([packed] * lax.axis_size('ctl')), 'ctl', 0, 0)  336 us
    all_to_all x1, waiting for transfers between devices, local(): received = lax.all_to_all(group_parts, 'ctl', 0, 0, tiled=True)  72.5 us
    ppermute x3, waiting for transfers between devices, swap(): return lax.ppermute(value, axis, [(0, 1), (1, 0)])  71.5 us
    all_to_all x1, starting transfers between devices, local(): received = lax.all_to_all(group_parts, 'ctl', 0, 0, tiled=True)  68.2 us
    dot_general x2, local copies, waits for them, and re-layouts, local(): jnp.dot(text_flat, pair_weight, preferred_element_type=jnp.float32)  20.7 us
  transfers between devices with their start and end apart: 8, of which 8 were waited for; matrix products, arithmetic and copies ran while one was open for 5% of the time, Pallas kernels for 0%

profile of v1, /device:TPU:69, one launch (start us, length us, event | category | flops | bytes accessed | tf_op | source)
XLA Modules:
  0.0 757.4 jit_solution(1432896113467647215)
XLA Ops:
  0.7 1.5 copy.20
  2.2 0.8 copy.38
  3.0 0.9 constant_dynamic-slice_fusion.2
  3.9 1.1 pad_maximum_fusion.1
  5.1 8.1 %stack.2 = bf16[32,96,3840]{2,1,0:T(8,128)(2,1)} broadcast(bf16[96,3840]{1,0:T(8,128)(2,1)S(1)} %pad_maximum_fusion.1), dimensions={1,2} | broadcast | bytes 24330240 | tf_op jit(solution)/shard_map/stack | solution.py:91
  13.2 8.3 %all-to-all-start = ((bf16[32,96,3840]{2,1,0:T(8,128)(2,1)}), bf16[32,96,3840]{2,1,0:T(8,128)(2,1)}, u32[]{:S(2)}, u32[]{:S(2)}) async-start(bf16[32,96,3840]{2,1,0:T(8,128)(2,1)} %stack.2), calls=%async_computation | async-start | bytes 47185920 | tf_op jit(solution)/shard_map/all_to_all | solution.py:91
  21.6 14.8 %gather_fusion.1 = bf16[512,3072]{1,0:T(8,128)(2,1)} fusion(bf16[2,256,3072]{2,1,0:T(8,128)(2,1)S(1)} %copy-done, s32[512]{0:T(512)S(1)} %bitcast.110), kind=kCustom, calls=%fused_computation.1 | custom fusion | bytes 6295552 | tf_op jit(solution)/shard_map/vmap(jit(_take))/gather | solution.py:72
  36.3 3.7 gather_fusion
  40.1 1.7 select_convert_fusion
  41.7 4.4 multiply_add_fusion
  46.1 0.6 fusion.1
  46.8 1.3 multiply_reduce_fusion
  48.1 0.6 copy-done.2
  48.7 3.6 add_convert_fusion
  52.3 336.1 %all-to-all-done = bf16[32,96,3840]{2,1,0:T(8,128)(2,1)} async-done(((bf16[32,96,3840]{2,1,0:T(8,128)(2,1)}), bf16[32,96,3840]{2,1,0:T(8,128)(2,1)}, u32[]{:S(2)}, u32[]{:S(2)}) %all-to-all-start) | async-done | bytes 23592992 | tf_op jit(solution)/shard_map/all_to_all | solution.py:91
  388.4 8.0 %slice_bitcast_fusion = bf16[1536,3072]{0,1:T(8,128)(2,1)} fusion(bf16[3072,3840]{1,0:T(8,128)(2,1)} %bitcast.10), kind=kLoop, calls=%fused_computation.3 | loop fusion | bytes 18874368 | tf_op jit(solution)/shard_map/dot_general | solution.py:99
  396.4 7.9 %fusion.46 = (bf16[3072,768]{1,0:T(8,128)(2,1)}, bf16[768,3072]{0,1:T(8,128)(2,1)}) fusion(bf16[3072,3840]{1,0:T(8,128)(2,1)} %bitcast.10), kind=kLoop, calls=%fused_computation.99 | loop fusion | bytes 18874368 | tf_op jit(solution)/shard_map/slice | solution.py:96
  404.4 12.6 %copy.21 = bf16[1536,3072]{1,0:T(8,128)(2,1)} copy(bf16[1536,3072]{0,1:T(8,128)(2,1)} %slice_bitcast_fusion) | data formatting | bytes 18874368 | tf_op jit(solution)/shard_map/dot_general | solution.py:99
  417.0 11.5 %fusion.4 = f32[2,384,2,6,128]{1,4,3,2,0:T(8,128)S(1)} fusion(bf16[2,6,128,3072,1]{3,2,1,0,4:T(8,128)(2,1)} %bitcast.114, bf16[2,384,3072]{2,1,0:T(8,128)(2,1)} %add_convert_fusion), kind=kOutput, calls=%fused_computation.14 | convolution fusion | flops 7247757312 | bytes 18874368 | tf_op jit(solution)/shard_map/dot_general | solution.py:99
  428.5 2.2 copy-done.9
  431.0 6.7 copy.22
  437.7 6.2 multiply_reduce_fusion.5
  443.9 0.9 fusion.22
  444.8 2.1 copy-done.4
  447.0 1.7 fusion.48
  448.7 10.0 %fusion.21 = bf16[2,256,6,128]{1,3,2,0:T(8,128)(2,1)S(1)} fusion(f32[2,6,256]{2,1,0:T(8,128)S(1)} %fusion.48, f32[2,384,2,6,128]{1,4,3,2,0:T(8,128)} %copy-done.9, f32[2,6,256,384]{3,2,1,0:T(8,128)} %copy-done.4), kind=kOutput, calls=%fused_computation.53 | convolution fusion | flops 308284800 | bytes 11415552 | tf_op jit(solution)/shard_map/bhij,bjhd->bihd/dot_general | solution.py:111
  458.7 0.8 copy.25
  459.7 3.1 convolution_convert_fusion.1
  462.8 0.3 collective-permute-start
  463.1 3.1 convolution_convert_fusion.2
  466.3 32.6 %collective-permute-done = bf16[512,1536]{1,0:T(8,128)(2,1)} collective-permute-done((bf16[512,1536]{1,0:T(8,128)(2,1)S(1)}, bf16[512,1536]{1,0:T(8,128)(2,1)}, u32[]{:S(2)}, u32[]{:S(2)}) %collective-permute-start) | collective-permute-done | bytes 1572896 | tf_op jit(solution)/shard_map/ppermute | solution.py:24
  498.9 1.8 convert_add_fusion.1
  500.8 4.9 fusion.27
  505.7 1.7 copy.27
  507.4 0.4 collective-permute-start.1
  507.8 0.8 copy-done.8
  508.5 33.9 %collective-permute-done.1 = bf16[512,1536]{0,1:T(8,128)(2,1)} collective-permute-done((bf16[512,1536]{0,1:T(8,128)(2,1)S(1)}, bf16[512,1536]{0,1:T(8,128)(2,1)}, u32[]{:S(2)}, u32[]{:S(2)}) %collective-permute-start.1) | collective-permute-done | bytes 1572896 | tf_op jit(solution)/shard_map/ppermute | solution.py:24
  542.4 3.3 maximum_select_fusion
  545.8 1.3 collective-permute-start.2
  547.1 8.6 %collective-permute-done.2 = bf16[512,3072]{0,1:T(8,128)(2,1)S(1)} collective-permute-done((bf16[512,3072]{0,1:T(8,128)(2,1)S(1)}, bf16[512,3072]{0,1:T(8,128)(2,1)S(1)}, u32[]{:S(2)}, u32[]{:S(2)}) %collective-permute-start.2) | collective-permute-done | bytes 3145760 | tf_op jit(solution)/shard_map/ppermute | solution.py:14
  555.7 0.4 broadcast_select_fusion
  556.1 6.1 fusion.18
  562.3 0.2 collective-permute-start.3
  562.6 2.0 collective-permute-done.3
  564.6 0.9 copy-done.12
  565.5 4.4 fusion.45
  569.9 5.4 all-reduce.1
  575.4 0.7 add_convert_fusion.1
  576.0 0.6 fusion.49
  576.6 0.4 collective-permute-start.4
  577.1 4.9 collective-permute-done.4
  582.0 0.7 fusion.10
  582.7 0.6 multiply_reduce_fusion.2
  583.4 1.0 copy-done.5
  584.4 5.3 all-reduce
  589.7 4.0 multiply_convert_fusion
  593.7 5.8 collective-permute-start.5
  599.5 1.5 constant_dynamic-slice_fusion.1
  601.0 1.4 collective-permute-done.5
  602.4 5.7 convolution_convert_fusion
  608.1 68.2 %all-to-all-start.1 = ((bf16[32,48,1536]{2,1,0:T(8,128)(2,1)}), bf16[32,48,1536]{2,1,0:T(8,128)(2,1)}, u32[]{:S(2)}, u32[]{:S(2)}) async-start(bf16[32,48,1536]{2,1,0:T(8,128)(2,1)} %bitcast.118), calls=%async_computation.1 | async-start | bytes 9437184 | tf_op jit(solution)/shard_map/all_to_all | solution.py:196
  676.3 4.7 select_bitcast_fusion
  680.9 72.5 %all-to-all-done.1 = bf16[32,48,1536]{2,1,0:T(8,128)(2,1)} async-done(((bf16[32,48,1536]{2,1,0:T(8,128)(2,1)}), bf16[32,48,1536]{2,1,0:T(8,128)(2,1)}, u32[]{:S(2)}, u32[]{:S(2)}) %all-to-all-start.1) | async-done | bytes 4718624 | tf_op jit(solution)/shard_map/all_to_all | solution.py:196
  753.4 3.7 convert_reduce_fusion
  (56 shorter events, 0.7 us)
Async XLA Ops:
  0.6 20.9 %copy-start = (bf16[2,256,3072]{2,1,0:T(8,128)(2,1)S(1)}, bf16[2,256,3072]{2,1,0:T(8,128)(2,1)}, u32[]{:S(2)}) copy-start(bf16[2,256,3072]{2,1,0:T(8,128)(2,1)} %param.14) | copy-start | bytes 9437188
  13.2 8.3 %copy-start.17 = (s32[2,256]{1,0:T(2,128)S(1)}, s32[2,256]{1,0:T(2,128)}, u32[]{:S(2)}) copy-start(s32[2,256]{1,0:T(2,128)} %param.15) | copy-start | bytes 6148
  13.2 375.2 %all-to-all-start = ((bf16[32,96,3840]{2,1,0:T(8,128)(2,1)}), bf16[32,96,3840]{2,1,0:T(8,128)(2,1)}, u32[]{:S(2)}, u32[]{:S(2)}) async-start(bf16[32,96,3840]{2,1,0:T(8,128)(2,1)} %stack.2), calls=%async_computation | async-start | bytes 47185920 | tf_op jit(solution)/shard_map/all_to_all | solution.py:91
  21.5 14.8 %copy-start.19 = (s32[2]{0:T(128)S(1)}, s32[2]{0:T(128)}, u32[]{:S(2)}) copy-start(s32[2]{0:T(128)} %param.17) | copy-start | bytes 28
  36.3 3.7 copy-start.18
  46.1 2.6 copy-start.2
  46.8 1.3 copy-start.15
  428.5 2.2 copy-start.9
  437.7 6.2 copy-start.10
  444.8 2.2 copy-start.4
  462.8 36.0 %collective-permute-start = (bf16[512,1536]{1,0:T(8,128)(2,1)S(1)}, bf16[512,1536]{1,0:T(8,128)(2,1)}, u32[]{:S(2)}, u32[]{:S(2)}) collective-permute-start(bf16[512,1536]{1,0:T(8,128)(2,1)S(1)} %convolution_convert_fusion.1), channel_id=1, source_target_pairs={{0,1},{1,0},{2,3},{3,2},{4,5},{5,4},{6,7},{7,6},{8,9},{9,8},{10,11... | collective-permute-start | bytes 4718600 | tf_op jit(solution)/shard_map/ppermute | solution.py:24
  500.7 4.9 copy-start.6
  507.4 1.1 copy-start.8
  507.4 35.0 %collective-permute-start.1 = (bf16[512,1536]{0,1:T(8,128)(2,1)S(1)}, bf16[512,1536]{0,1:T(8,128)(2,1)}, u32[]{:S(2)}, u32[]{:S(2)}) collective-permute-start(bf16[512,1536]{0,1:T(8,128)(2,1)S(1)} %copy.27), channel_id=1, source_target_pairs={{0,1},{1,0},{2,3},{3,2},{4,5},{5,4},{6,7},{7,6},{8,9},{9,8},{10,11... | collective-permute-start | bytes 4718600 | tf_op jit(solution)/shard_map/ppermute | solution.py:24
  545.8 9.9 %collective-permute-start.2 = (bf16[512,3072]{0,1:T(8,128)(2,1)S(1)}, bf16[512,3072]{0,1:T(8,128)(2,1)S(1)}, u32[]{:S(2)}, u32[]{:S(2)}) collective-permute-start(bf16[512,3072]{0,1:T(8,128)(2,1)S(1)} %maximum_select_fusion), channel_id=1, source_target_pairs={{0,2},{1,3},{4,6},{5,7},{8,10},{9,11},{12,14},{13,15},{16,18},{17,... | collective-permute-start | bytes 9437192 | tf_op jit(solution)/shard_map/ppermute | solution.py:14
  556.1 6.2 copy-start.7
  556.1 6.4 copy-start.16
  562.3 2.4 copy-start.11
  562.3 2.4 collective-permute-start.3
  564.6 0.9 copy-start.12
  569.9 19.8 %copy-start.3 = (f32[2,256,1536]{2,1,0:T(8,128)}, f32[2,256,1536]{2,1,0:T(8,128)S(1)}, u32[]{:S(2)}) copy-start(f32[2,256,1536]{2,1,0:T(8,128)S(1)} %get-tuple-element.8) | copy-start | bytes 9437188
  569.9 6.1 copy-start.13
  575.4 1.7 copy-start.14
  576.6 5.4 collective-permute-start.4
  582.7 1.7 copy-start.5
  593.7 8.7 %collective-permute-start.5 = (bf16[512,1536]{1,0:T(8,128)(2,1)}, bf16[512,1536]{1,0:T(8,128)(2,1)S(1)}, u32[]{:S(2)}, u32[]{:S(2)}) collective-permute-start(bf16[512,1536]{1,0:T(8,128)(2,1)} %bitcast.41), channel_id=1, source_target_pairs={{2,0},{3,1},{6,4},{7,5},{10,8},{11,9},{14,12},{15,13},{18,16},{19,... | collective-permute-start | bytes 4718600 | tf_op jit(solution)/shard_map/ppermute | solution.py:14
  608.1 145.4 %all-to-all-start.1 = ((bf16[32,48,1536]{2,1,0:T(8,128)(2,1)}), bf16[32,48,1536]{2,1,0:T(8,128)(2,1)}, u32[]{:S(2)}, u32[]{:S(2)}) async-start(bf16[32,48,1536]{2,1,0:T(8,128)(2,1)} %bitcast.118), calls=%async_computation.1 | async-start | bytes 9437184 | tf_op jit(solution)/shard_map/all_to_all | solution.py:196
  676.2 81.0 %copy-start.1 = (bf16[2,256,3072]{2,1,0:T(8,128)(2,1)S(1)}, bf16[2,256,3072]{2,1,0:T(8,128)(2,1)}, u32[]{:S(2)}) copy-start(bf16[2,256,3072]{2,1,0:T(8,128)(2,1)} %param.14) | copy-start | bytes 9437188
